TPU v7x, 32 devices: a whole 2x2x4 slice. The times are simulated.
32 devices in a mesh: row: 2 (over x), col: 4 (over z), tok: 4 (over y, core).
Axes of the slice: x: 2, y: 2, z: 4, core: 2. Of those that a mesh axis runs over, the one named last changes fastest.
Arguments:
- activations: bfloat16 [4096, 2048], P(('row', 'col', 'tok')), may hold values from -6 to 6
- norm_gain: float32 [2048], replicated, may hold values from 0.1 to 1.9
- routes: int32 [4096, 8], P(('row', 'col', 'tok')), may hold values from 0 to 127, all different within a row; in each aligned block of 128 rows (0 to 127, 128 to 255, ...) at most 10 rows name the same one
- route_weights: float32 [4096, 8], P(('row', 'col', 'tok')), may hold values from 0.05 to 1
- gate_up_weight: bfloat16 [128, 2, 768, 2048], P(('row', 'col'), None, 'tok'), may hold values from -0.125 to 0.125
- down_weight: bfloat16 [128, 768, 2048], P(('row', 'col'), 'tok'), may hold values from -0.21875 to 0.21875
Outputs:
- expert_mix: bfloat16 [4096, 2048], P(('row', 'col', 'tok'))
Inputs may be any that keep to these rules, and one draw needn't show every extreme that they name: `routes`: within the rows of one device no expert is named by more than 10 rows, a bound that some block reaches.
All inputs are finite; a program needn't handle non-finite values.
Results may differ from a plain program's by a relative error of at most 0.0085.
Values may be sent and summed in bfloat16 or wider, within the bound.
No kernel may reach another device: no remote copies, remote signals or barrier semaphores. Data moves between devices by JAX's collectives and lax.ppermute only.
A program may use at most 384 MiB of HBM per device.

v0:
```python
import math
import jax
import jax.numpy as jnp
from jax import lax
from jax.sharding import PartitionSpec as P

CAP = 10
PIECES = 4
EPSILON = 1e-06
ALL = ("row", "col", "tok")


def rank_in_block(block_routes, experts):
    onehot = (block_routes[:, None] == jnp.arange(experts, dtype=jnp.int32)[None, :]).astype(
        jnp.int32
    )
    before = jnp.cumsum(onehot, axis=0) - onehot
    return jnp.sum(before * onehot, axis=1)


def rms_normed(activations, norm_gain):
    values = activations.astype(jnp.float32)
    scale = lax.rsqrt(jnp.mean(values * values, axis=-1, keepdims=True) + EPSILON)
    return (values * scale * norm_gain).astype(jnp.bfloat16)


def local(activations, norm_gain, routes, route_weights, gate_up_weight, down_weight):
    count, features = activations.shape
    chosen = routes.shape[1]
    holding = gate_up_weight.shape[0]
    row_count = lax.axis_size("row")
    col_count = lax.axis_size("col")
    tok_count = lax.axis_size("tok")
    owners = row_count * col_count
    experts = holding * owners
    devices = owners * tok_count
    owner = lax.axis_index("row") * col_count + lax.axis_index("col")
    assert count < 256
    normed = rms_normed(activations, norm_gain)
    gates = route_weights / jnp.sum(route_weights, axis=1, keepdims=True)
    flat_routes = routes.reshape(-1)
    target = flat_routes * CAP + rank_in_block(flat_routes, experts)
    token_ids = jnp.arange(count * chosen, dtype=jnp.int32) // chosen
    source = jnp.full((experts * CAP,), count, jnp.int32).at[target].set(token_ids)
    extra = -(-(experts * CAP) // features)
    extra = -(-extra // 8) * 8
    stride = count + extra
    table_rows = jnp.zeros((extra * features,), jnp.bfloat16)
    table_rows = table_rows.at[: experts * CAP].set(source.astype(jnp.bfloat16))
    packed = jnp.concatenate([normed, table_rows.reshape(extra, features)], axis=0)
    every = lax.all_gather(packed, ALL, axis=0, tiled=True)
    tables = every.reshape(devices, stride, features)[:, count:, :].reshape(devices, -1)
    tables = lax.dynamic_slice_in_dim(
        tables[:, : experts * CAP], owner * holding * CAP, holding * CAP, axis=1
    ).astype(jnp.int32)
    rows = tables + (jnp.arange(devices, dtype=jnp.int32) * stride)[:, None]
    rows = rows.reshape(owners, tok_count, holding, CAP).transpose(2, 1, 0, 3).reshape(-1)
    rows = rows.reshape(holding, -1)
    pieces = math.gcd(holding, PIECES)
    width = holding // pieces
    returned = []
    sums = []
    for piece in range(pieces):
        span = slice(piece * width, (piece + 1) * width)
        picked = jnp.take(every, rows[span].reshape(-1), axis=0, mode="clip")
        picked = picked.reshape(width, tok_count * owners * CAP, features)
        both = jnp.einsum(
            "jrd,jgfd->jrgf", picked, gate_up_weight[span], preferred_element_type=jnp.float32
        )
        hidden = (jax.nn.silu(both[:, :, 0, :]) * both[:, :, 1, :]).astype(jnp.bfloat16)
        partial = jnp.einsum(
            "jrf,jfd->jrd", hidden, down_weight[span], preferred_element_type=jnp.float32
        )
        partial = partial.astype(jnp.bfloat16)
        if sums:
            partial, _ = lax.optimization_barrier((partial, (sums[-1], returned[:-1])))
        sums.append(lax.psum_scatter(partial, "tok", scatter_dimension=1, tiled=True))
        summed = sums[-1].reshape(width, owners, CAP, features).transpose(1, 0, 2, 3)
        summed = summed.reshape(owners, width * CAP, features)
        returned.append(
            lax.all_to_all(summed, ("row", "col"), split_axis=0, concat_axis=0, tiled=True)
        )
    returned = jnp.concatenate(returned, axis=1)
    picked_back = jnp.take(returned.reshape(experts * CAP, features), target, axis=0)
    picked_back = picked_back.reshape(count, chosen, features)
    mixed = jnp.einsum("tk,tkd->td", gates, picked_back.astype(jnp.float32))
    return mixed.astype(jnp.bfloat16)


def solution(mesh):
    in_specs = (
        P(("row", "col", "tok"), None),
        P(),
        P(("row", "col", "tok"), None),
        P(("row", "col", "tok"), None),
        P(("row", "col"), None, "tok", None),
        P(("row", "col"), "tok", None),
    )
    out_specs = P(("row", "col", "tok"), None)
    return jax.shard_map(local, mesh=mesh, in_specs=in_specs, out_specs=out_specs, check_vma=False)
```

profile of v0, /device:TPU:0, one launch (start us, length us, event | category | flops | bytes accessed | tf_op | source)
XLA Modules:
  0.0 457.8 jit_solution(16420601011597710427)
XLA Ops:
  6.5 0.7 broadcast_multiply_fusion
  7.3 0.8 copy.68
  8.3 1.2 fusion.23
  10.6 4.3 scatter_custom_fusion
  15.2 0.9 pad_maximum_fusion.1
  16.2 122.6 %all-gather.2.cloned.1.call-done = bf16[4352,2048]{1,0:T(8,128)(2,1)} async-done(((bf16[136,2048]{1,0:T(8,128)(2,1)}), bf16[4352,2048]{1,0:T(8,128)(2,1)}) %all-gather.2.cloned.1.call-update) | async-done | bytes 17825808 | tf_op jit(solution)/shard_map/all_gather | solution.py:51
  138.8 1.3 slice.123
  140.1 0.6 copy.108
  141.2 19.2 %gather_fusion = bf16[1280,2048]{1,0:T(8,128)(2,1)} fusion(bf16[4352,2048]{1,0:T(8,128)(2,1)} %all-gather.2.cloned.1.call-done, s32[2048]{0:T(1024)S(1)} %pad_clamp_fusion.3), kind=kCustom, calls=%fused_computation | custom fusion | bytes 10490880 | tf_op jit(solution)/shard_map/jit(_take)/gather | solution.py:65
  160.4 7.8 %fusion.6 = f32[4,320,2,192]{1,3,2,0:T(8,128)S(1)} fusion(bf16[4,320,2048,1]{2,1,3,0:T(8,128)(2,1)} %bitcast.124, bf16[16,2,192,2048]{3,2,1,0:T(8,128)(2,1)} %param.12), kind=kOutput, calls=%fused_computation.12 | convolution fusion | flops 2013265920 | bytes 13500416 | tf_op jit(solution)/shard_map/jrd,jgfd->jrgf/dot_general | solution.py:67
  168.2 5.8 %convolution_convert_fusion.3 = bf16[4,320,2048]{2,1,0:T(8,128)(2,1)} fusion(bf16[16,192,2048]{2,1,0:T(8,128)(2,1)} %param.13, f32[4,320,2,192]{1,3,2,0:T(8,128)S(1)} %fusion.6), kind=kOutput, calls=%fused_computation.21 | convolution fusion | flops 1010728960 | bytes 10354688 | tf_op jit(solution)/shard_map/jrf,jfd->jrd/dot_general | solution.py:71
  174.2 16.3 %fusion.49 = (bf16[4,2,192,2048]{3,2,1,0:T(8,128)(2,1)}, bf16[4,2,192,2048]{3,2,1,0:T(8,128)(2,1)}, bf16[4,2,192,2048]{3,2,1,0:T(8,128)(2,1)}) fusion(bf16[16,2,192,2048]{3,2,1,0:T(8,128)(2,1)} %param.12), kind=kLoop, calls=%fused_computation.91 | loop fusion | bytes 37748736 | tf_op jit(solution)/shard_map/slice | solution.py:68
  190.6 20.0 %gather_fusion.1 = bf16[1280,2048]{1,0:T(8,128)(2,1)} fusion(bf16[4352,2048]{1,0:T(8,128)(2,1)} %all-gather.2.cloned.1.call-done, s32[2048]{0:T(1024)S(1)} %pad_clamp_fusion.2), kind=kCustom, calls=%fused_computation.1 | custom fusion | bytes 10490880 | tf_op jit(solution)/shard_map/jit(_take)/gather | solution.py:65
  210.7 7.8 %fusion.4 = f32[4,320,2,192]{1,3,0,2:T(8,128)S(1)} fusion(bf16[4,320,2048,1]{2,1,0,3:T(8,128)(2,1)} %bitcast.122, bf16[4,2,192,2048]{3,2,1,0:T(8,128)(2,1)} %get-tuple-element.23), kind=kOutput, calls=%fused_computation.10 | convolution fusion | flops 2013265920 | bytes 13500416 | tf_op jit(solution)/shard_map/jrd,jgfd->jrgf/dot_general | solution.py:67
  218.5 5.8 %convolution_convert_fusion.2 = bf16[4,320,2048]{2,1,0:T(8,128)(2,1)} fusion(bf16[16,192,2048]{2,1,0:T(8,128)(2,1)} %param.13, f32[4,320,2,192]{1,3,0,2:T(8,128)S(1)} %fusion.4), kind=kOutput, calls=%fused_computation.20 | convolution fusion | flops 1010728960 | bytes 10354688 | tf_op jit(solution)/shard_map/jrf,jfd->jrd/dot_general | solution.py:71
  224.3 1.3 copy-done.2
  225.6 1.0 copy.77
  226.6 0.7 copy.78
  227.3 1.8 copy.79
  229.1 5.0 %all-to-all-start = ((bf16[8,40,2048]{2,1,0:T(8,128)(2,1)}), bf16[8,40,2048]{2,1,0:T(8,128)(2,1)S(1)}, u32[]{:S(2)}, u32[]{:S(2)}) async-start(bf16[8,40,2048]{2,1,0:T(8,128)(2,1)} %copy.79), calls=%async_computation.1 | async-start | bytes 2621440 | tf_op jit(solution)/shard_map/all_to_all | solution.py:81
  234.5 20.5 %gather_fusion.2 = bf16[1280,2048]{1,0:T(8,128)(2,1)} fusion(bf16[4352,2048]{1,0:T(8,128)(2,1)} %all-gather.2.cloned.1.call-done, s32[2048]{0:T(1024)S(1)} %pad_clamp_fusion.1), kind=kCustom, calls=%fused_computation.2 | custom fusion | bytes 10490880 | tf_op jit(solution)/shard_map/jit(_take)/gather | solution.py:65
  255.0 7.9 %fusion.2 = f32[4,320,2,192]{1,3,0,2:T(8,128)S(1)} fusion(bf16[4,320,2048,1]{2,1,0,3:T(8,128)(2,1)} %bitcast.123, bf16[4,2,192,2048]{3,2,1,0:T(8,128)(2,1)} %get-tuple-element.25), kind=kOutput, calls=%fused_computation.8 | convolution fusion | flops 2013265920 | bytes 13500416 | tf_op jit(solution)/shard_map/jrd,jgfd->jrgf/dot_general | solution.py:67
  262.9 5.9 %convolution_convert_fusion.1 = bf16[4,320,2048]{2,1,0:T(8,128)(2,1)} fusion(bf16[16,192,2048]{2,1,0:T(8,128)(2,1)} %param.13, f32[4,320,2,192]{1,3,0,2:T(8,128)S(1)} %fusion.2), kind=kOutput, calls=%fused_computation.19 | convolution fusion | flops 1010728960 | bytes 10354688 | tf_op jit(solution)/shard_map/jrf,jfd->jrd/dot_general | solution.py:71
  268.8 9.1 %reduce-scatter.7.cloned.1.call-done = bf16[4,80,2048]{2,1,0:T(8,128)(2,1)} async-done(((bf16[4,320,2048]{2,1,0:T(8,128)(2,1)}), bf16[4,80,2048]{2,1,0:T(8,128)(2,1)}) %reduce-scatter.7.cloned.1.call-update) | async-done | bytes 1310736 | tf_op jit(solution)/shard_map/reduce_scatter | solution.py:77
  277.9 1.3 copy-done.1
  279.2 1.0 copy.83
  280.2 0.7 copy.84
  280.9 1.8 copy.85
  282.7 5.5 %all-to-all-start.1 = ((bf16[8,40,2048]{2,1,0:T(8,128)(2,1)}), bf16[8,40,2048]{2,1,0:T(8,128)(2,1)S(1)}, u32[]{:S(2)}, u32[]{:S(2)}) async-start(bf16[8,40,2048]{2,1,0:T(8,128)(2,1)} %copy.85), calls=%async_computation.3 | async-start | bytes 2621440 | tf_op jit(solution)/shard_map/all_to_all | solution.py:81
  288.2 0.4 reduce-scatter.11.cloned.1.call-start
  288.8 20.2 %gather_fusion.3 = bf16[1280,2048]{1,0:T(8,128)(2,1)} fusion(bf16[4352,2048]{1,0:T(8,128)(2,1)} %all-gather.2.cloned.1.call-done, s32[2048]{0:T(1024)S(1)} %pad_clamp_fusion), kind=kCustom, calls=%fused_computation.3 | custom fusion | bytes 10490880 | tf_op jit(solution)/shard_map/jit(_take)/gather | solution.py:65
  309.0 7.9 %fusion = f32[4,320,2,192]{1,3,0,2:T(8,128)S(1)} fusion(bf16[4,320,2048,1]{2,1,0,3:T(8,128)(2,1)} %bitcast.121, bf16[4,2,192,2048]{3,2,1,0:T(8,128)(2,1)} %get-tuple-element.24), kind=kOutput, calls=%fused_computation.6 | convolution fusion | flops 2013265920 | bytes 13500416 | tf_op jit(solution)/shard_map/jrd,jgfd->jrgf/dot_general | solution.py:67
  316.9 5.9 %convolution_convert_fusion = bf16[4,320,2048]{2,1,0:T(8,128)(2,1)} fusion(bf16[16,192,2048]{2,1,0:T(8,128)(2,1)} %param.13, f32[4,320,2,192]{1,3,0,2:T(8,128)S(1)} %fusion), kind=kOutput, calls=%fused_computation.18 | convolution fusion | flops 1010728960 | bytes 10354688 | tf_op jit(solution)/shard_map/jrf,jfd->jrd/dot_general | solution.py:71
  322.8 8.8 %reduce-scatter.9.cloned.1.call-done = bf16[4,80,2048]{2,1,0:T(8,128)(2,1)} async-done(((bf16[4,320,2048]{2,1,0:T(8,128)(2,1)}), bf16[4,80,2048]{2,1,0:T(8,128)(2,1)}) %reduce-scatter.9.cloned.1.call-update) | async-done | bytes 1310736 | tf_op jit(solution)/shard_map/reduce_scatter | solution.py:77
  331.7 2.3 copy.89
  334.0 0.7 copy.90
  334.7 1.9 copy.91
  336.6 5.8 %all-to-all-start.2 = ((bf16[8,40,2048]{2,1,0:T(8,128)(2,1)}), bf16[8,40,2048]{2,1,0:T(8,128)(2,1)}, u32[]{:S(2)}, u32[]{:S(2)}) async-start(bf16[8,40,2048]{2,1,0:T(8,128)(2,1)} %copy.91), calls=%async_computation.5 | async-start | bytes 2621440 | tf_op jit(solution)/shard_map/all_to_all | solution.py:81
  342.4 43.3 %reduce-scatter.11.cloned.1.call-done = bf16[4,80,2048]{2,1,0:T(8,128)(2,1)} async-done(((bf16[4,320,2048]{2,1,0:T(8,128)(2,1)}), bf16[4,80,2048]{2,1,0:T(8,128)(2,1)}) %reduce-scatter.11.cloned.1.call-update) | async-done | bytes 1310736 | tf_op jit(solution)/shard_map/reduce_scatter | solution.py:77
  385.6 2.3 copy.95
  388.0 0.7 copy.96
  388.7 1.8 copy.97
  390.5 5.5 %all-to-all-start.3 = ((bf16[8,40,2048]{2,1,0:T(8,128)(2,1)}), bf16[8,40,2048]{2,1,0:T(8,128)(2,1)}, u32[]{:S(2)}, u32[]{:S(2)}) async-start(bf16[8,40,2048]{2,1,0:T(8,128)(2,1)} %copy.97), calls=%async_computation.7 | async-start | bytes 2621440 | tf_op jit(solution)/shard_map/all_to_all | solution.py:81
  396.5 31.9 %all-to-all-done.3 = bf16[8,40,2048]{2,1,0:T(8,128)(2,1)} async-done(((bf16[8,40,2048]{2,1,0:T(8,128)(2,1)}), bf16[8,40,2048]{2,1,0:T(8,128)(2,1)}, u32[]{:S(2)}, u32[]{:S(2)}) %all-to-all-start.3) | async-done | bytes 1310752 | tf_op jit(solution)/shard_map/all_to_all | solution.py:81
  428.4 6.0 %pad_maximum_fusion = bf16[8,160,2048]{2,1,0:T(8,128)(2,1)} fusion(bf16[8,40,2048]{2,1,0:T(8,128)(2,1)} %all-to-all-done.3, bf16[8,40,2048]{2,1,0:T(8,128)(2,1)} %all-to-all-done.2, bf16[8,40,2048]{2,1,0:T(8,128)(2,1)S(1)} %all-to-all-done.1, bf16[8,40,2048]{2,1,0:T(8,128)(2,1)S(1)} %all-to-all-done), kind=kLoop, calls=%fused_computation.14 | loop fusion | flops 20971520 | bytes 10485760 | tf_op jit(solution)/shard_map/concatenate | solution.py:83
  434.4 12.0 %gather_fusion.4 = bf16[1024,2048]{1,0:T(8,128)(2,1)} fusion(bf16[1280,2048]{1,0:T(8,128)(2,1)} %bitcast.120, s32[1024]{0:T(1024)S(1)} %broadcast_clamp_fusion), kind=kCustom, calls=%fused_computation.4 | custom fusion | bytes 8392704 | tf_op jit(solution)/shard_map/jit(_take)/gather | solution.py:84
  446.4 3.5 fusion.8
  449.9 1.1 copy.116
  (67 shorter events, 3.5 us)
Async XLA Ops:
  6.5 8.4 %copy-start = (bf16[128,2048]{1,0:T(8,128)(2,1)S(1)}, bf16[128,2048]{1,0:T(8,128)(2,1)}, u32[]{:S(2)}) copy-start(bf16[128,2048]{1,0:T(8,128)(2,1)} %param.8) | copy-start | bytes 1572868
  6.5 8.5 %copy-start.5 = (f32[2048]{0:T(1024)S(1)}, f32[2048]{0:T(1024)}, u32[]{:S(2)}) copy-start(f32[2048]{0:T(1024)} %param.9) | copy-start | bytes 24580
  6.5 132.2 %all-gather.2.cloned.1.call-start = ((), (), s32[]{:S(2)}) async-start(), calls=%async_computation.8 | async-start | bytes 18382848 | tf_op jit(solution)/shard_map/all_gather | solution.py:51
  16.1 208.2 %reduce-scatter.5.cloned.1.call-start = ((), (), s32[]{:S(2)}) async-start(), calls=%async_computation.9 | async-start | bytes 6553600 | tf_op jit(solution)/shard_map/reduce_scatter | solution.py:77
  174.0 103.9 %reduce-scatter.7.cloned.1.call-start = ((), (), s32[]{:S(2)}) async-start(), calls=%async_computation.10 | async-start | bytes 6553600 | tf_op jit(solution)/shard_map/reduce_scatter | solution.py:77
  224.2 1.3 copy-start.2
  229.1 39.7 %all-to-all-start = ((bf16[8,40,2048]{2,1,0:T(8,128)(2,1)}), bf16[8,40,2048]{2,1,0:T(8,128)(2,1)S(1)}, u32[]{:S(2)}, u32[]{:S(2)}) async-start(bf16[8,40,2048]{2,1,0:T(8,128)(2,1)} %copy.79), calls=%async_computation.1 | async-start | bytes 2621440 | tf_op jit(solution)/shard_map/all_to_all | solution.py:81
  234.1 97.6 %reduce-scatter.9.cloned.1.call-start = ((), (), s32[]{:S(2)}) async-start(), calls=%async_computation.11 | async-start | bytes 6553600 | tf_op jit(solution)/shard_map/reduce_scatter | solution.py:77
  277.8 1.3 copy-start.1
  282.7 40.1 %all-to-all-start.1 = ((bf16[8,40,2048]{2,1,0:T(8,128)(2,1)}), bf16[8,40,2048]{2,1,0:T(8,128)(2,1)S(1)}, u32[]{:S(2)}, u32[]{:S(2)}) async-start(bf16[8,40,2048]{2,1,0:T(8,128)(2,1)} %copy.85), calls=%async_computation.3 | async-start | bytes 2621440 | tf_op jit(solution)/shard_map/all_to_all | solution.py:81
  288.2 97.4 %reduce-scatter.11.cloned.1.call-start = ((), (), s32[]{:S(2)}) async-start(), calls=%async_computation.12 | async-start | bytes 6553600 | tf_op jit(solution)/shard_map/reduce_scatter | solution.py:77
  336.6 53.9 %all-to-all-start.2 = ((bf16[8,40,2048]{2,1,0:T(8,128)(2,1)}), bf16[8,40,2048]{2,1,0:T(8,128)(2,1)}, u32[]{:S(2)}, u32[]{:S(2)}) async-start(bf16[8,40,2048]{2,1,0:T(8,128)(2,1)} %copy.91), calls=%async_computation.5 | async-start | bytes 2621440 | tf_op jit(solution)/shard_map/all_to_all | solution.py:81
  388.0 8.2 %copy-start.4 = (f32[128,8]{0,1:T(8,128)S(1)}, f32[128,8]{0,1:T(8,128)}, u32[]{:S(2)}) copy-start(f32[128,8]{0,1:T(8,128)} %param.11) | copy-start | bytes 12292
  388.0 8.4 %copy-start.3 = (s32[128,8]{0,1:T(8,128)S(1)}, s32[128,8]{0,1:T(8,128)}, u32[]{:S(2)}) copy-start(s32[128,8]{0,1:T(8,128)} %param.10) | copy-start | bytes 12292
  390.5 37.9 %all-to-all-start.3 = ((bf16[8,40,2048]{2,1,0:T(8,128)(2,1)}), bf16[8,40,2048]{2,1,0:T(8,128)(2,1)}, u32[]{:S(2)}, u32[]{:S(2)}) async-start(bf16[8,40,2048]{2,1,0:T(8,128)(2,1)} %copy.97), calls=%async_computation.7 | async-start | bytes 2621440 | tf_op jit(solution)/shard_map/all_to_all | solution.py:81
Sparse Core Ops, SparseCore 0:
  16.2 122.5 all-gather.1
  174.1 49.5 reduce-scatter.4
  226.4 51.4 reduce-scatter.6
  280.2 51.3 reduce-scatter.8
  334.2 51.3 reduce-scatter.10
where the time goes:
time: 467 us; the launch traced here: 458 us
  waiting for transfers between devices  216 us (46%)
  local copies, waits for them, and re-layouts  138 us (30%)
  matrix products  58.2 us (12%)
  starting transfers between devices  22.7 us (5%)
  between operations  13.7 us (3%)
  other arithmetic  9.89 us (2%)
    all_gather x1, waiting for transfers between devices, local(): every = lax.all_gather(packed, ALL, axis=0, tiled=True)  123 us
    gather x4, local copies, waits for them, and re-layouts, local(): picked = jnp.take(every, rows[span].reshape(-1), axis=0, mode='clip')  79.9 us
    reduce_scatter x4, waiting for transfers between devices, local(): lax.psum_scatter(partial, 'tok', scatter_dimension=1, tiled=True)  61.2 us
    all_to_all x4, waiting for transfers between devices, local(): lax.all_to_all(summed, ('row', 'col'), split_axis=0, concat_axis=0, tiled...  31.9 us
    dot_general x4, matrix products, local(): jnp.einsum('jrd,jgfd->jrgf', picked, gate_up_weight[span], preferred_elem...  31.4 us
    dot_general x4, matrix products, local(): jnp.einsum('jrf,jfd->jrd', hidden, down_weight[span], preferred_element_t...  23.3 us
    all_to_all x4, starting transfers between devices, local(): lax.all_to_all(summed, ('row', 'col'), split_axis=0, concat_axis=0, tiled...  21.7 us
    slice x1, local copies, waits for them, and re-layouts, local(): gate_up_weight[span]  16.3 us
  transfers between devices with their start and end apart: 9, of which 5 were waited for; matrix products, arithmetic and copies ran while one was open for 30% of the time, Pallas kernels for 0%

commit v1 on v0

--- a/solution.py
+++ b/solution.py
@@ -3,11 +3,36 @@
 import jax.numpy as jnp
 from jax import lax
 from jax.sharding import PartitionSpec as P
+from jax.lax import axis_index, ppermute, psum
 
 CAP = 10
 PIECES = 4
 EPSILON = 1e-06
 ALL = ("row", "col", "tok")
+
+
+def step_on_the_record(inputs, at_axis):
+    all_rows = list(inputs.shape[1:])
+    all_rows[at_axis] *= inputs.shape[0]
+    return jnp.moveaxis(inputs, 0, at_axis).reshape(all_rows)
+
+
+def _launch_ends(tile_in, shard_axis):
+    degree = psum(1, axis_name=shard_axis)
+    x_next = tile_in[None]
+    for pp in range(degree.bit_length() - 1):
+        carry_in = 1 << pp
+        local_out = ppermute(x_next, shard_axis, [(w, w ^ carry_in) for w in range(degree)])
+        top = jnp.stack([x_next, local_out])
+        val2 = axis_index(shard_axis)
+        taken_in = val2 >> pp & 1
+        x_next = jnp.where(taken_in == 0, top, top[::-1]).reshape(-1, *tile_in.shape)
+    return x_next
+
+
+def derive_object(d0, raw, chunk):
+    v_now = _launch_ends(raw, chunk)
+    return step_on_the_record(v_now, d0)
 
 
 def rank_in_block(block_routes, experts):
@@ -48,7 +73,7 @@
     table_rows = jnp.zeros((extra * features,), jnp.bfloat16)
     table_rows = table_rows.at[: experts * CAP].set(source.astype(jnp.bfloat16))
     packed = jnp.concatenate([normed, table_rows.reshape(extra, features)], axis=0)
-    every = lax.all_gather(packed, ALL, axis=0, tiled=True)
+    every = derive_object(0, packed, ALL)
     tables = every.reshape(devices, stride, features)[:, count:, :].reshape(devices, -1)
     tables = lax.dynamic_slice_in_dim(
         tables[:, : experts * CAP], owner * holding * CAP, holding * CAP, axis=1

time: 467 us -> 866 us (1.85)
  waiting for transfers between devices: 216 us -> 554 us
  other arithmetic: 9.89 us -> 55.7 us
  starting transfers between devices: 22.7 us -> 31.7 us
    ppermute x0 -> x5, waiting for transfers between devices: none -> 458 us  [_launch_ends(): ppermute(x_next, shard_axis, [(w, w ^ carry_in) for w in range(degree)])]
    all_gather x1 -> x0, waiting for transfers between devices: 123 us -> none  [local(): every = lax.all_gather(packed, ALL, axis=0, tiled=True)]
    select_n x0 -> x4, other arithmetic: none -> 26.8 us  [_launch_ends(): jnp.where(taken_in == 0, top, top[::-1]).reshape(-1, *tile_in.shape)]
    another operation x3 -> x10, other arithmetic: 0.27 us -> 19.5 us  [the longest x7 19.3 us: _launch_ends(): top = jnp.stack([x_next, local_out])]
    ppermute x0 -> x5, starting transfers between devices: none -> 8.88 us  [_launch_ends(): ppermute(x_next, shard_axis, [(w, w ^ carry_in) for w in range(degree)])]
  transfers between devices with their start and end apart: 9 -> 13, of which waited for: 5 -> 10; matrix products, arithmetic and copies ran while one was open for 30% -> 16% of each run, Pallas kernels for 0% -> 0%
where the time goes in v1:
time: 866 us; the launch traced here: 857 us
  waiting for transfers between devices  554 us (64%)
  local copies, waits for them, and re-layouts  143 us (17%)
  matrix products  58.3 us (7%)
  other arithmetic  55.7 us (6%)
  starting transfers between devices  31.7 us (4%)
  between operations  14 us (2%)
    ppermute x5, waiting for transfers between devices, _launch_ends(): ppermute(x_next, shard_axis, [(w, w ^ carry_in) for w in range(degree)])  458 us
    gather x4, local copies, waits for them, and re-layouts, local(): picked = jnp.take(every, rows[span].reshape(-1), axis=0, mode='clip')  80.1 us
    reduce_scatter x4, waiting for transfers between devices, local(): lax.psum_scatter(partial, 'tok', scatter_dimension=1, tiled=True)  64.1 us
    all_to_all x4, waiting for transfers between devices, local(): lax.all_to_all(summed, ('row', 'col'), split_axis=0, concat_axis=0, tiled...  31.8 us
    dot_general x4, matrix products, local(): jnp.einsum('jrd,jgfd->jrgf', picked, gate_up_weight[span], preferred_elem...  31.5 us
    select_n x4, other arithmetic, _launch_ends(): jnp.where(taken_in == 0, top, top[::-1]).reshape(-1, *tile_in.shape)  26.8 us
    dot_general x4, matrix products, local(): jnp.einsum('jrf,jfd->jrd', hidden, down_weight[span], preferred_element_t...  23.3 us
    all_to_all x4, starting transfers between devices, local(): lax.all_to_all(summed, ('row', 'col'), split_axis=0, concat_axis=0, tiled...  22.3 us
  transfers between devices with their start and end apart: 13, of which 10 were waited for; matrix products, arithmetic and copies ran while one was open for 16% of the time, Pallas kernels for 0%

profile of v1, /device:TPU:0, one launch (start us, length us, event | category | flops | bytes accessed | tf_op | source)
XLA Modules:
  0.0 856.8 jit_solution(4059496062673325609)
XLA Ops:
  11.2 4.3 scatter_custom_fusion
  17.1 1.6 collective-permute-done
  19.3 3.0 collective-permute-start.1
  22.2 24.9 %collective-permute-done.1 = bf16[2,136,2048]{2,1,0:T(8,128)(2,1)S(1)} collective-permute-done((bf16[2,136,2048]{2,1,0:T(8,128)(2,1)S(1)}, bf16[2,136,2048]{2,1,0:T(8,128)(2,1)S(1)}, u32[]{:S(2)}, u32[]{:S(2)}) %collective-permute-start.1) | collective-permute-done | bytes 1114144 | tf_op jit(solution)/shard_map/ppermute | solution.py:25
  47.8 1.9 collective-permute-start.2
  49.7 48.3 %collective-permute-done.2 = bf16[4,136,2048]{2,1,0:T(8,128)(2,1)} collective-permute-done((bf16[4,136,2048]{2,1,0:T(8,128)(2,1)S(1)}, bf16[4,136,2048]{2,1,0:T(8,128)(2,1)}, u32[]{:S(2)}, u32[]{:S(2)}) %collective-permute-start.2) | collective-permute-done | bytes 2228256 | tf_op jit(solution)/shard_map/ppermute | solution.py:25
  98.0 2.0 pad_maximum_fusion.3
  100.0 3.4 reverse_select_fusion.2
  103.4 2.5 collective-permute-start.3
  105.9 191.0 %collective-permute-done.3 = bf16[8,136,2048]{2,1,0:T(8,128)(2,1)} collective-permute-done((bf16[8,136,2048]{2,1,0:T(8,128)(2,1)}, bf16[8,136,2048]{2,1,0:T(8,128)(2,1)}, u32[]{:S(2)}, u32[]{:S(2)}) %collective-permute-start.3) | collective-permute-done | bytes 4456480 | tf_op jit(solution)/shard_map/ppermute | solution.py:25
  296.9 7.9 pad_maximum_fusion.1
  304.8 15.0 %reverse_select_fusion.1 = bf16[2,8,136,2048]{3,2,1,0:T(8,128)(2,1)} fusion(bf16[2,8,136,2048]{3,2,1,0:T(8,128)(2,1)} %pad_maximum_fusion.1, pred[]{:T(512)S(6)} %eq.46), kind=kLoop, calls=%fused_computation.8 | loop fusion | flops 4456448 | bytes 17825792 | tf_op jit(solution)/shard_map/jit(_where)/select_n | solution.py:29
  320.9 192.2 %collective-permute-done.4 = bf16[16,136,2048]{2,1,0:T(8,128)(2,1)} collective-permute-done((bf16[16,136,2048]{2,1,0:T(8,128)(2,1)}, bf16[16,136,2048]{2,1,0:T(8,128)(2,1)}, u32[]{:S(2)}, u32[]{:S(2)}) %collective-permute-start.4) | collective-permute-done | bytes 8912928 | tf_op jit(solution)/shard_map/ppermute | solution.py:25
  513.1 8.5 pad_maximum_fusion
  521.6 7.9 reverse_select_fusion
  529.5 6.1 copy-done
  536.8 19.2 %gather_fusion = bf16[1280,2048]{1,0:T(8,128)(2,1)} fusion(bf16[4352,2048]{1,0:T(8,128)(2,1)} %bitcast.140, s32[2048]{0:T(1024)S(1)} %pad_clamp_fusion.3), kind=kCustom, calls=%fused_computation | custom fusion | bytes 10490880 | tf_op jit(solution)/shard_map/jit(_take)/gather | solution.py:90
  556.0 7.8 fusion.6
  563.8 5.7 convolution_convert_fusion.3
  569.6 16.0 %fusion.53 = (bf16[4,2,192,2048]{3,2,1,0:T(8,128)(2,1)}, bf16[4,2,192,2048]{3,2,1,0:T(8,128)(2,1)}, bf16[4,2,192,2048]{3,2,1,0:T(8,128)(2,1)}) fusion(bf16[16,2,192,2048]{3,2,1,0:T(8,128)(2,1)} %param.12), kind=kLoop, calls=%fused_computation.105 | loop fusion | bytes 37748736 | tf_op jit(solution)/shard_map/slice | solution.py:93
  585.8 20.1 %gather_fusion.1 = bf16[1280,2048]{1,0:T(8,128)(2,1)} fusion(bf16[4352,2048]{1,0:T(8,128)(2,1)} %bitcast.141, s32[2048]{0:T(1024)S(1)} %pad_clamp_fusion.2), kind=kCustom, calls=%fused_computation.1 | custom fusion | bytes 10490880 | tf_op jit(solution)/shard_map/jit(_take)/gather | solution.py:90
  605.9 7.9 fusion.4
  613.8 5.8 convolution_convert_fusion.2
  619.6 2.8 reduce-scatter.5.cloned.1.call-done
  622.5 1.3 copy-done.3
  625.5 1.8 copy.79
  627.3 5.5 all-to-all-start
  633.2 20.5 %gather_fusion.2 = bf16[1280,2048]{1,0:T(8,128)(2,1)} fusion(bf16[4352,2048]{1,0:T(8,128)(2,1)} %bitcast.142, s32[2048]{0:T(1024)S(1)} %pad_clamp_fusion.1), kind=kCustom, calls=%fused_computation.2 | custom fusion | bytes 10490880 | tf_op jit(solution)/shard_map/jit(_take)/gather | solution.py:90
  653.7 7.9 fusion.2
  661.6 5.9 convolution_convert_fusion.1
  667.5 9.1 %reduce-scatter.7.cloned.1.call-done = bf16[4,80,2048]{2,1,0:T(8,128)(2,1)} async-done(((bf16[4,320,2048]{2,1,0:T(8,128)(2,1)}), bf16[4,80,2048]{2,1,0:T(8,128)(2,1)}) %reduce-scatter.7.cloned.1.call-update) | async-done | bytes 1310736 | tf_op jit(solution)/shard_map/reduce_scatter | solution.py:102
  679.6 1.8 copy.85
  681.4 5.5 all-to-all-start.1
  687.3 20.3 %gather_fusion.3 = bf16[1280,2048]{1,0:T(8,128)(2,1)} fusion(bf16[4352,2048]{1,0:T(8,128)(2,1)} %bitcast.143, s32[2048]{0:T(1024)S(1)} %pad_clamp_fusion), kind=kCustom, calls=%fused_computation.3 | custom fusion | bytes 10490880 | tf_op jit(solution)/shard_map/jit(_take)/gather | solution.py:90
  707.7 7.9 fusion
  715.6 5.9 convolution_convert_fusion
  721.5 9.0 %reduce-scatter.9.cloned.1.call-done = bf16[4,80,2048]{2,1,0:T(8,128)(2,1)} async-done(((bf16[4,320,2048]{2,1,0:T(8,128)(2,1)}), bf16[4,80,2048]{2,1,0:T(8,128)(2,1)}) %reduce-scatter.9.cloned.1.call-update) | async-done | bytes 1310736 | tf_op jit(solution)/shard_map/reduce_scatter | solution.py:102
  730.5 2.3 copy.89
  733.6 1.8 copy.91
  735.4 5.8 all-to-all-start.2
  741.2 43.2 %reduce-scatter.11.cloned.1.call-done = bf16[4,80,2048]{2,1,0:T(8,128)(2,1)} async-done(((bf16[4,320,2048]{2,1,0:T(8,128)(2,1)}), bf16[4,80,2048]{2,1,0:T(8,128)(2,1)}) %reduce-scatter.11.cloned.1.call-update) | async-done | bytes 1310736 | tf_op jit(solution)/shard_map/reduce_scatter | solution.py:102
  784.5 2.3 copy.95
  787.6 1.8 copy.97
  789.4 5.5 all-to-all-start.3
  795.4 31.8 %all-to-all-done.3 = bf16[8,40,2048]{2,1,0:T(8,128)(2,1)} async-done(((bf16[8,40,2048]{2,1,0:T(8,128)(2,1)}), bf16[8,40,2048]{2,1,0:T(8,128)(2,1)}, u32[]{:S(2)}, u32[]{:S(2)}) %all-to-all-start.3) | async-done | bytes 1310752 | tf_op jit(solution)/shard_map/all_to_all | solution.py:106
  827.2 6.0 pad_maximum_fusion.2
  833.2 12.0 %gather_fusion.4 = bf16[1024,2048]{1,0:T(8,128)(2,1)} fusion(bf16[1280,2048]{1,0:T(8,128)(2,1)} %bitcast.144, s32[1024]{0:T(1024)S(1)} %broadcast_clamp_fusion), kind=kCustom, calls=%fused_computation.4 | custom fusion | bytes 8392704 | tf_op jit(solution)/shard_map/jit(_take)/gather | solution.py:109
  845.3 3.5 fusion.8
  (92 shorter events, 18.5 us)
Async XLA Ops:
  6.5 9.0 %copy-start.1 = (bf16[128,2048]{1,0:T(8,128)(2,1)S(1)}, bf16[128,2048]{1,0:T(8,128)(2,1)}, u32[]{:S(2)}) copy-start(bf16[128,2048]{1,0:T(8,128)(2,1)} %param.8) | copy-start | bytes 1572868
  6.5 615.9 %reduce-scatter.5.cloned.1.call-start = ((), (), s32[]{:S(2)}) async-start(), calls=%async_computation.8 | async-start | bytes 6553600 | tf_op jit(solution)/shard_map/reduce_scatter | solution.py:102
  10.6 0.6 copy-start.4
  11.2 4.3 copy-start.7
  16.6 2.1 collective-permute-start
  19.3 27.8 %collective-permute-start.1 = (bf16[2,136,2048]{2,1,0:T(8,128)(2,1)S(1)}, bf16[2,136,2048]{2,1,0:T(8,128)(2,1)S(1)}, u32[]{:S(2)}, u32[]{:S(2)}) collective-permute-start(bf16[2,136,2048]{2,1,0:T(8,128)(2,1)S(1)} %get-tuple-element.27), channel_id=1, source_target_pairs={{0,2},{1,3},{2,0},{3,1},{4,6},{5,7},{6,4},{7,5},{8,10},{9,11},{10,... | collective-permute-start | bytes 3342344 | tf_op jit(solution)/shard_map/ppermute | solution.py:25
  47.8 50.1 %collective-permute-start.2 = (bf16[4,136,2048]{2,1,0:T(8,128)(2,1)S(1)}, bf16[4,136,2048]{2,1,0:T(8,128)(2,1)}, u32[]{:S(2)}, u32[]{:S(2)}) collective-permute-start(bf16[4,136,2048]{2,1,0:T(8,128)(2,1)S(1)} %bitcast.147), channel_id=1, source_target_pairs={{0,4},{1,5},{2,6},{3,7},{4,0},{5,1},{6,2},{7,3},{8,12},{9,13},{10,... | collective-permute-start | bytes 6684680 | tf_op jit(solution)/shard_map/ppermute | solution.py:25
  103.4 193.5 %collective-permute-start.3 = (bf16[8,136,2048]{2,1,0:T(8,128)(2,1)}, bf16[8,136,2048]{2,1,0:T(8,128)(2,1)}, u32[]{:S(2)}, u32[]{:S(2)}) collective-permute-start(bf16[8,136,2048]{2,1,0:T(8,128)(2,1)} %bitcast.16), channel_id=1, source_target_pairs={{0,8},{1,9},{2,10},{3,11},{4,12},{5,13},{6,14},{7,15},{8,0},{9,1},... | collective-permute-start | bytes 13369352 | tf_op jit(solution)/shard_map/ppermute | solution.py:25
  319.8 193.3 %collective-permute-start.4 = (bf16[16,136,2048]{2,1,0:T(8,128)(2,1)}, bf16[16,136,2048]{2,1,0:T(8,128)(2,1)}, u32[]{:S(2)}, u32[]{:S(2)}) collective-permute-start(bf16[16,136,2048]{2,1,0:T(8,128)(2,1)} %bitcast.145), channel_id=1, source_target_pairs={{0,16},{1,17},{2,18},{3,19},{4,20},{5,21},{6,22},{7,23},{8,24},{9,... | collective-permute-start | bytes 26738696 | tf_op jit(solution)/shard_map/ppermute | solution.py:25
  529.5 6.1 copy-start
  569.6 107.0 %reduce-scatter.7.cloned.1.call-start = ((), (), s32[]{:S(2)}) async-start(), calls=%async_computation.9 | async-start | bytes 6553600 | tf_op jit(solution)/shard_map/reduce_scatter | solution.py:102
  622.4 1.3 copy-start.3
  627.3 40.2 %all-to-all-start = ((bf16[8,40,2048]{2,1,0:T(8,128)(2,1)}), bf16[8,40,2048]{2,1,0:T(8,128)(2,1)S(1)}, u32[]{:S(2)}, u32[]{:S(2)}) async-start(bf16[8,40,2048]{2,1,0:T(8,128)(2,1)} %copy.79), calls=%async_computation.1 | async-start | bytes 2621440 | tf_op jit(solution)/shard_map/all_to_all | solution.py:106
  632.8 97.7 %reduce-scatter.9.cloned.1.call-start = ((), (), s32[]{:S(2)}) async-start(), calls=%async_computation.10 | async-start | bytes 6553600 | tf_op jit(solution)/shard_map/reduce_scatter | solution.py:102
  676.5 1.3 copy-start.2
  681.4 40.1 %all-to-all-start.1 = ((bf16[8,40,2048]{2,1,0:T(8,128)(2,1)}), bf16[8,40,2048]{2,1,0:T(8,128)(2,1)S(1)}, u32[]{:S(2)}, u32[]{:S(2)}) async-start(bf16[8,40,2048]{2,1,0:T(8,128)(2,1)} %copy.85), calls=%async_computation.3 | async-start | bytes 2621440 | tf_op jit(solution)/shard_map/all_to_all | solution.py:106
  686.9 97.6 %reduce-scatter.11.cloned.1.call-start = ((), (), s32[]{:S(2)}) async-start(), calls=%async_computation.11 | async-start | bytes 6553600 | tf_op jit(solution)/shard_map/reduce_scatter | solution.py:102
  735.4 54.0 %all-to-all-start.2 = ((bf16[8,40,2048]{2,1,0:T(8,128)(2,1)}), bf16[8,40,2048]{2,1,0:T(8,128)(2,1)}, u32[]{:S(2)}, u32[]{:S(2)}) async-start(bf16[8,40,2048]{2,1,0:T(8,128)(2,1)} %copy.91), calls=%async_computation.5 | async-start | bytes 2621440 | tf_op jit(solution)/shard_map/all_to_all | solution.py:106
  786.8 8.1 copy-start.5
  786.8 8.2 copy-start.9
  786.8 8.4 copy-start.6
  786.8 8.6 %copy-start.8 = (s32[1024,1]{0,1:T(1,128)S(1)}, s32[1024,1]{0,1:T(1,128)}, u32[]{:S(2)}) copy-start(s32[1024,1]{0,1:T(1,128)} %copy-done.7) | copy-start | bytes 12292
  789.4 37.9 %all-to-all-start.3 = ((bf16[8,40,2048]{2,1,0:T(8,128)(2,1)}), bf16[8,40,2048]{2,1,0:T(8,128)(2,1)}, u32[]{:S(2)}, u32[]{:S(2)}) async-start(bf16[8,40,2048]{2,1,0:T(8,128)(2,1)} %copy.97), calls=%async_computation.7 | async-start | bytes 2621440 | tf_op jit(solution)/shard_map/all_to_all | solution.py:106
Sparse Core Ops, SparseCore 0:
  569.7 52.7 reduce-scatter.4
  625.1 51.3 reduce-scatter.6
  679.1 51.3 reduce-scatter.8
  733.0 51.3 reduce-scatter.10
